TPU v7x, 32 devices: a whole 2x2x4 slice. The times are simulated.
32 devices in a mesh: req: 4 (over y, x), exp: 4 (over z), ffn: 2 (over core).
Axes of the slice: x: 2, y: 2, z: 4, core: 2. Of those that a mesh axis runs over, the one named last changes fastest.
Arguments:
- residual: bfloat16 [2048, 2048], P(('req', 'exp')), may hold values from -5 to 5
- queries: bfloat16 [2048, 4608], P(('req', 'exp'), 'ffn'), may hold values from -30 to 30
- new_latent: bfloat16 [2048, 576], P(('req', 'exp')), may hold values from -6 to 6
- cache_pool: bfloat16 [512, 9216], P(('req', 'exp')), may hold values from -5 to 5
- page_table: int32 [8, 64], replicated, may hold values from 0 to 511, as said below
- cached_len: int32 [8], replicated, may hold values from 0 to 1024
- tenant_start: int32 [8], replicated, may hold values from 0 to 512, as said below
- routes: int32 [2048, 6], P(('req', 'exp')), may hold values from 0 to 31, all different within a row; in each aligned block of 64 rows (0 to 63, 64 to 127, ...) at most 16 rows name the same one
- value_up: bfloat16 [512, 1024], P(None, 'ffn'), may hold values from -0.25 to 0.25
- out_proj: bfloat16 [1024, 2048], P('ffn'), may hold values from -0.1875 to 0.1875
- norm_gain: bfloat16 [2048], replicated, may hold values from 0.099609375 to 1.8984375
- router: bfloat16 [2048, 32], replicated, may hold values from -0.125 to 0.125
- gate_weight: bfloat16 [32, 2048, 1408], P('exp', None, 'ffn'), may hold values from -0.125 to 0.125
- up_weight: bfloat16 [32, 2048, 1408], P('exp', None, 'ffn'), may hold values from -0.125 to 0.125
- down_weight: bfloat16 [32, 1408, 2048], P('exp', 'ffn'), may hold values from -0.15625 to 0.15625
Outputs:
- hidden_out: bfloat16 [2048, 2048], P(('req', 'exp'), 'ffn')
- moe_out: bfloat16 [2048, 2048], P(('req', 'exp'), 'ffn')
Inputs may be any that keep to these rules, and one draw needn't show every extreme that they name: `page_table`: row i lists, in order, the pool pages of request i's cache; the 2 requests of group g = i // 2 use pool pages g * 2 * 64 to (g + 1) * 2 * 64 - 1, each exactly once. tenant_start[i] is at most half of cached_len[i]. `routes`: A row names 6 different experts; in each aligned block of 64 rows at most 16 rows name the same expert.
All inputs are finite; a program needn't handle non-finite values.
Results may differ from a plain program's by a relative error of at most 0.025.
Values may be sent and summed in bfloat16 or wider, within the bound.
No kernel may reach another device: no remote copies, remote signals or barrier semaphores. Data moves between devices by JAX's collectives and lax.ppermute only.
A program may use at most 128 MiB of HBM per device.

v0:
```python
import jax
import jax.numpy as jnp
from jax import lax
from jax.sharding import PartitionSpec as P

LATENT = 512
ROPE_DIM = 64
HEAD_DIM = 128
QKD = 576
EXPERTS = 32
TOP = 6
CAPACITY = 16
REQ_GRP = 2
CMAX = 1024
BLOCK_ROWS = 64
EPSILON = 1e-06
NEG_FILL = -1e30


def local(
    residual,
    queries,
    new_latent,
    cache_pool,
    page_table,
    cached_len,
    tenant_start,
    routes,
    value_up,
    out_proj,
    norm_gain,
    router,
    gate_weight,
    up_weight,
    down_weight,
):
    exp_size = lax.axis_size("exp")
    ffn_size = lax.axis_size("ffn")
    req_index = lax.axis_index("req")
    exp_index = lax.axis_index("exp")
    ffn_index = lax.axis_index("ffn")
    token_rows = residual.shape[0]
    feature_count = residual.shape[1]
    fresh_len = token_rows * exp_size // REQ_GRP
    first_token = (req_index * exp_size + exp_index) * token_rows
    request = first_token // fresh_len
    offset = first_token - request * fresh_len
    pool_pages = cache_pool.shape[0]
    page_width = cache_pool.shape[1]
    latent_pages = token_rows * QKD // page_width
    route_count = token_rows * TOP
    route_pages = -(-route_count // page_width)
    route_rows = jnp.pad(
        routes.reshape(route_count).astype(jnp.bfloat16),
        (0, route_pages * page_width - route_count),
    ).reshape(route_pages, page_width)
    packed_rows = pool_pages + latent_pages + route_pages
    share_rows = -(-packed_rows // ffn_size)
    packed = jnp.concatenate(
        [
            cache_pool,
            new_latent.reshape(latent_pages, page_width),
            route_rows,
            jnp.zeros((share_rows * ffn_size - packed_rows, page_width), jnp.bfloat16),
        ],
        axis=0,
    )
    share = lax.dynamic_slice_in_dim(packed, ffn_index * share_rows, share_rows, 0)
    gathered = lax.all_gather(share, ("exp", "ffn"), axis=0, tiled=False)
    gathered = gathered.reshape(exp_size, ffn_size * share_rows, page_width)
    stride = ffn_size * share_rows
    group_rows = exp_size * token_rows
    routes_all = (
        gathered[:, pool_pages + latent_pages : packed_rows]
        .reshape(exp_size, route_pages * page_width)[:, :route_count]
        .reshape(group_rows, TOP)
        .astype(jnp.int32)
    )
    flat_pages = gathered.reshape(exp_size * stride, page_width)
    pool_base = req_index * exp_size * pool_pages
    page_rows = page_table[request] - pool_base
    cached_rows = page_rows // pool_pages * stride + page_rows % pool_pages
    local_request = request - req_index * REQ_GRP
    fresh_devices = fresh_len // token_rows
    fresh_index = lax.broadcasted_iota(jnp.int32, (fresh_devices, latent_pages), 0)
    fresh_rows = (
        (local_request * fresh_devices + fresh_index) * stride
        + pool_pages
        + lax.broadcasted_iota(jnp.int32, (fresh_devices, latent_pages), 1)
    ).reshape(fresh_devices * latent_pages)
    key_rows = jnp.concatenate([cached_rows, fresh_rows], axis=0)
    all_keys = jnp.take(flat_pages, key_rows, axis=0).reshape(CMAX + fresh_len, QKD)
    heads_here = queries.shape[1] // QKD
    query_heads = queries.reshape(token_rows, heads_here, QKD)
    scale_factor = (HEAD_DIM + ROPE_DIM) ** (-0.5)
    scores = (
        jnp.einsum("thd,kd->thk", query_heads, all_keys, preferred_element_type=jnp.float32)
        * scale_factor
    )
    key_pos = lax.broadcasted_iota(jnp.int32, (1, CMAX + fresh_len), 1)
    tok_pos = offset + lax.broadcasted_iota(jnp.int32, (token_rows, 1), 0)
    cached_ok = (key_pos >= tenant_start[request]) & (key_pos < cached_len[request])
    fresh_ok = (key_pos >= CMAX) & (key_pos - CMAX <= tok_pos)
    visible = cached_ok | fresh_ok
    scores = jnp.where(visible[:, None, :], scores, NEG_FILL)
    top_score = jnp.max(scores, axis=2, keepdims=True)
    weights = jnp.exp(scores - top_score)
    attn_probs = (weights / jnp.sum(weights, axis=2, keepdims=True)).astype(jnp.bfloat16)
    latent_out = jnp.einsum(
        "thk,kl->thl", attn_probs, all_keys[:, :LATENT], preferred_element_type=jnp.float32
    ).astype(jnp.bfloat16)
    value_heads = value_up.reshape(LATENT, heads_here, HEAD_DIM)
    head_out = jnp.einsum(
        "thl,lhd->thd", latent_out, value_heads, preferred_element_type=jnp.float32
    )
    head_out = head_out.astype(jnp.bfloat16).reshape(token_rows, heads_here * HEAD_DIM)
    partial_value = jnp.dot(head_out, out_proj, preferred_element_type=jnp.float32)
    column_count = feature_count // ffn_size
    attn_cols = lax.psum_scatter(
        partial_value.astype(jnp.bfloat16), "ffn", scatter_dimension=1, tiled=True
    ).astype(jnp.float32)
    residual_cols = lax.dynamic_slice_in_dim(residual, ffn_index * column_count, column_count, 1)
    hidden_out = (residual_cols.astype(jnp.float32) + attn_cols).astype(jnp.bfloat16)
    hidden_wide = hidden_out.astype(jnp.float32)
    square_sum = lax.psum(jnp.sum(hidden_wide * hidden_wide, axis=1, keepdims=True), "ffn")
    mean_square = square_sum / feature_count
    gain_cols = lax.dynamic_slice_in_dim(norm_gain, ffn_index * column_count, column_count, 0)
    normed_cols = (
        hidden_wide * lax.rsqrt(mean_square + EPSILON) * gain_cols.astype(jnp.float32)
    ).astype(jnp.bfloat16)
    normed_half = lax.all_gather(normed_cols, "exp", axis=0, tiled=True)
    normed_all = lax.all_gather(normed_half, "ffn", axis=1, tiled=True)
    expert_ids = lax.broadcasted_iota(jnp.int32, (1, 1, EXPERTS), 2)
    route_hot = routes_all[:, :, None] == expert_ids
    blocks = group_rows // BLOCK_ROWS
    pair_count = BLOCK_ROWS * TOP
    pair_hot = route_hot.reshape(blocks, pair_count, EXPERTS).astype(jnp.bfloat16)
    earlier = (
        lax.broadcasted_iota(jnp.int32, (pair_count, pair_count), 1)
        < lax.broadcasted_iota(jnp.int32, (pair_count, pair_count), 0)
    ).astype(jnp.bfloat16)
    before = jnp.einsum("pq,bqx->bpx", earlier, pair_hot, preferred_element_type=jnp.float32)
    rank = jnp.sum(before * pair_hot.astype(jnp.float32), axis=2).astype(jnp.int32)
    block_base = lax.broadcasted_iota(jnp.int32, (blocks, 1), 0) * CAPACITY
    slot_index = (rank + block_base).reshape(group_rows, TOP)
    slot_count = blocks * CAPACITY
    local_count = gate_weight.shape[0]
    total_slots = local_count * slot_count
    local_expert = routes_all - exp_index * local_count
    is_local = (local_expert >= 0) & (local_expert < local_count)
    target = jnp.where(is_local, local_expert * slot_count + slot_index, -1)
    logits = jnp.dot(normed_all, router, preferred_element_type=jnp.float32)
    chosen = jnp.sum(jnp.where(route_hot, logits[:, None, :], 0.0), axis=2)
    raised = jnp.exp(chosen)
    gate_weights = raised / jnp.sum(raised, axis=1, keepdims=True)
    slot_ids = lax.broadcasted_iota(jnp.int32, (1, 1, total_slots), 2)
    slot_hit = target[:, :, None] == slot_ids
    combine = jnp.any(slot_hit, axis=1).astype(jnp.bfloat16)
    slot_weight = jnp.sum(jnp.where(slot_hit, gate_weights[:, :, None], 0.0), axis=(0, 1))
    dispatch_ids = lax.broadcasted_iota(jnp.int32, (total_slots, 1, 1), 0)
    dispatch = jnp.any(target[None, :, :] == dispatch_ids, axis=2).astype(jnp.bfloat16)
    grouped = jnp.dot(dispatch, normed_all, preferred_element_type=jnp.float32).astype(jnp.bfloat16)
    grouped = grouped.reshape(local_count, slot_count, feature_count)
    gate_part = jnp.einsum("jmd,jdf->jmf", grouped, gate_weight, preferred_element_type=jnp.float32)
    up_part = jnp.einsum("jmd,jdf->jmf", grouped, up_weight, preferred_element_type=jnp.float32)
    active = (jax.nn.silu(gate_part) * up_part).astype(jnp.bfloat16)
    outputs = jnp.einsum("jmf,jfd->jmd", active, down_weight, preferred_element_type=jnp.float32)
    weighted = (outputs.reshape(total_slots, feature_count) * slot_weight[:, None]).astype(
        jnp.bfloat16
    )
    mixture = jnp.dot(combine, weighted, preferred_element_type=jnp.float32).astype(jnp.bfloat16)
    moe_cols = lax.psum_scatter(mixture, "ffn", scatter_dimension=1, tiled=True)
    moe_out = lax.psum_scatter(moe_cols, "exp", scatter_dimension=0, tiled=True)
    return (hidden_out, moe_out)


def solution(mesh):
    in_specs = (
        P(("req", "exp"), None),
        P(("req", "exp"), "ffn"),
        P(("req", "exp"), None),
        P(("req", "exp"), None),
        P(),
        P(),
        P(),
        P(("req", "exp"), None),
        P(None, "ffn"),
        P("ffn", None),
        P(),
        P(),
        P("exp", None, "ffn"),
        P("exp", None, "ffn"),
        P("exp", "ffn", None),
    )
    out_specs = (P(("req", "exp"), "ffn"), P(("req", "exp"), "ffn"))
    return jax.shard_map(local, mesh=mesh, in_specs=in_specs, out_specs=out_specs, check_vma=False)
```

profile of v0, /device:TPU:0, one launch (start us, length us, event | category | flops | bytes accessed | tf_op | source)
XLA Modules:
  0.0 243.3 jit_solution(17411121236919590765)
XLA Ops:
  7.2 1.2 copy.43
  9.8 2.3 fusion.36
  12.5 1.2 dynamic_slice.19
  13.7 1.2 dynamic_slice.20
  16.3 1.3 copy.55
  18.3 1.3 iota_compare_fusion.6
  20.7 35.9 %all-gather.10.cloned.1.call-done = bf16[8,21,9216]{2,1,0:T(8,128)(2,1)} async-done(((bf16[1,21,9216]{2,1,0:T(8,128)(2,1)}), bf16[8,21,9216]{2,1,0:T(8,128)(2,1)}) %all-gather.10.cloned.1.call-update) | async-done | bytes 3096592 | tf_op jit(solution)/shard_map/all_gather | solution.py:69
  56.6 4.8 %reshape.369 = bf16[168,9216]{1,0:T(8,128)(2,1)} reshape(bf16[8,21,9216]{2,1,0:T(8,128)(2,1)} %all-gather.10.cloned.1.call-done) | data formatting | bytes 6193152
  61.4 6.3 %gather_fusion = bf16[80,9216]{1,0:T(8,128)(2,1)} fusion(bf16[168,9216]{1,0:T(8,128)(2,1)} %reshape.369, s32[1024]{0:T(1024)S(1)} %pad_clamp_fusion), kind=kCustom, calls=%fused_computation | custom fusion | bytes 2949440 | tf_op jit(solution)/shard_map/jit(_take)/gather | solution.py:92
  67.7 2.7 %broadcast_select_fusion = bf16[80,9216]{1,0:T(8,128)(2,1)} fusion(bf16[80,9216]{1,0:T(8,128)(2,1)} %gather_fusion, pred[80]{0:T(512)(128)(4,1)S(1)} %compare_and_fusion), kind=kLoop, calls=%fused_computation.21 | loop fusion | flops 737280 | bytes 2949200 | tf_op jit(solution)/shard_map/jit(_take)/select_n | solution.py:92
  70.3 3.9 %gather.7 = bf16[1280,576]{1,0:T(8,128)(2,1)} reshape(bf16[80,9216]{1,0:T(8,128)(2,1)} %gather_fusion) | data formatting | bytes 2949120 | tf_op jit(solution)/shard_map/jit(_take)/gather | solution.py:92
  74.2 3.9 %select_n.117 = bf16[1280,576]{1,0:T(8,128)(2,1)} reshape(bf16[80,9216]{1,0:T(8,128)(2,1)} %broadcast_select_fusion) | data formatting | bytes 2949120 | tf_op jit(solution)/shard_map/jit(_take)/select_n | solution.py:92
  78.1 2.6 %fusion.6 = f32[128,4,1280]{0,2,1:T(8,128)S(1)} fusion(bf16[128,4,576]{0,2,1:T(8,128)(2,1)S(1)} %bitcast.75, bf16[1280,576]{1,0:T(8,128)(2,1)} %select_n.117, pred[128,1280]{0,1:T(8,128)(4,1)S(1)} %and_or_fusion), kind=kOutput, calls=%fused_computation.13 | convolution fusion | flops 756285440 | bytes 4849664 | tf_op jit(solution)/shard_map/thd,kd->thk/dot_general | solution.py:97
  80.8 1.5 copy-done.3
  82.9 4.4 %fusion.23 = bf16[4,128,128]{1,2,0:T(8,128)(2,1)S(1)} fusion(bf16[512,4,128]{0,2,1:T(8,128)(2,1)S(1)} %bitcast.76, bf16[1280,576]{1,0:T(8,128)(2,1)} %gather.7, pred[1280]{0:T(1024)(128)(4,1)S(1)} %broadcast_in_dim.81, f32[128,4]{0,1:T(4,128)S(1)} %fusion.49, f32[128,4,1280]{0,2,1:T(8,128)} %copy-done.3), kind=kOutput, calls=%fused_computation.32 | convolution fusion | flops 741148416 | bytes 7212288 | tf_op jit(solution)/shard_map/thl,lhd->thd/dot_general | solution.py:113
  87.3 1.3 convolution_convert_fusion.2
  88.8 6.7 %reduce-scatter.4.cloned.1.call-done = bf16[128,1024]{1,0:T(8,128)(2,1)} async-done(((bf16[128,2048]{1,0:T(8,128)(2,1)}), bf16[128,1024]{1,0:T(8,128)(2,1)}) %reduce-scatter.4.cloned.1.call-update) | async-done | bytes 262160 | tf_op jit(solution)/shard_map/reduce_scatter | solution.py:119
  96.6 2.5 %psum.7 = f32[128,1]{0,1:T(1,128)S(1)} all-reduce(f32[128,1]{0,1:T(1,128)S(1)} %bitcast.79), channel_id=1, replica_groups=mesh['req'=4,'exp'=4,'ffn'=2] {'ffn'}, use_global_device_ids=true, to_apply=%region_7.8 | all-reduce | flops 128 | bytes 1024 | tf_op jit(solution)/shard_map/psum | solution.py:125
  100.0 29.2 %all-gather.6.cloned.1.call-done = bf16[512,1024]{1,0:T(8,128)(2,1)} async-done(((bf16[128,1024]{1,0:T(8,128)(2,1)}), bf16[512,1024]{1,0:T(8,128)(2,1)}) %all-gather.6.cloned.1.call-update) | async-done | bytes 1048592 | tf_op jit(solution)/shard_map/all_gather | solution.py:131
  129.4 4.7 %reshape.351 = bf16[4,42,9216]{2,1,0:T(8,128)(2,1)} reshape(bf16[8,21,9216]{2,1,0:T(8,128)(2,1)} %all-gather.10.cloned.1.call-done) | data formatting | bytes 6193152 | tf_op jit(solution)/shard_map/reshape | solution.py:70
  136.5 2.3 fusion.2
  138.8 1.4 fusion.1
  140.8 2.3 fusion.51
  143.2 1.7 select_reduce_fusion
  145.0 3.9 %convolution_convert_fusion = bf16[1024,2048]{1,0:T(8,128)(2,1)S(1)} fusion(pred[1024,512]{1,0:T(8,128)(4,1)S(1)} %fusion.2, bf16[512,2048]{1,0:T(8,128)(2,1)} %all-gather.8.cloned.1.call-done), kind=kOutput, calls=%fused_computation.9 | convolution fusion | flops 2149580800 | bytes 6815744 | tf_op jit(solution)/shard_map/dot_general | solution.py:162
  148.9 2.0 copy-done.2
  150.9 12.3 %fusion.50 = f32[8,128,704]{1,2,0:T(8,128)} fusion(bf16[8,128,2048]{2,1,0:T(8,128)(2,1)S(1)} %bitcast.73, bf16[8,2048,704]{1,2,0:T(8,128)(2,1)} %param.27), kind=kOutput, calls=%fused_computation.89 | convolution fusion | flops 2952790016 | bytes 30146560 | tf_op jit(solution)/shard_map/jmd,jdf->jmf/dot_general | solution.py:164
  163.2 23.6 %fusion.8 = f32[8,128,2048]{2,1,0:T(8,128)} fusion(bf16[8,704,2048]{2,1,0:T(8,128)(2,1)} %param.29, f32[8,128,704]{1,2,0:T(8,128)} %fusion.50, bf16[8,128,2048]{2,1,0:T(8,128)(2,1)} %bitcast.74, bf16[8,2048,704]{1,2,0:T(8,128)(2,1)} %param.28), kind=kOutput, calls=%fused_computation.19 | convolution fusion | flops 5909905408 | bytes 61603840 | tf_op jit(solution)/shard_map/jmf,jfd->jmd/dot_general | solution.py:167
  186.7 3.9 %fusion.3 = bf16[1024,2048]{1,0:T(8,128)(2,1)S(1)} fusion(f32[8,128,2048]{2,1,0:T(8,128)} %fusion.8, f32[1024]{0:T(1024)S(1)} %select_reduce_fusion), kind=kLoop, calls=%fused_computation.8 | loop fusion | flops 4194304 | bytes 12587008 | tf_op jit(solution)/shard_map/convert_element_type | solution.py:168
  190.6 3.7 %convolution_convert_fusion.1 = bf16[512,2048]{1,0:T(8,128)(2,1)} fusion(pred[512,1024]{1,0:T(8,128)(4,1)S(1)} %fusion.1, bf16[1024,2048]{1,0:T(8,128)(2,1)S(1)} %fusion.3), kind=kOutput, calls=%fused_computation.15 | convolution fusion | flops 2148532224 | bytes 6815744 | tf_op jit(solution)/shard_map/dot_general | solution.py:171
  194.5 10.9 %reduce-scatter.6.cloned.1.call-done = bf16[512,1024]{1,0:T(8,128)(2,1)} async-done(((bf16[512,2048]{1,0:T(8,128)(2,1)}), bf16[512,1024]{1,0:T(8,128)(2,1)}) %reduce-scatter.6.cloned.1.call-update) | async-done | bytes 1048592 | tf_op jit(solution)/shard_map/reduce_scatter | solution.py:172
  205.4 31.1 %reduce-scatter.8.cloned.1.call-done = bf16[128,1024]{1,0:T(8,128)(2,1)} async-done(((bf16[512,1024]{1,0:T(8,128)(2,1)}), bf16[128,1024]{1,0:T(8,128)(2,1)}) %reduce-scatter.8.cloned.1.call-update) | async-done | bytes 262160 | tf_op jit(solution)/shard_map/reduce_scatter | solution.py:173
  (74 shorter events, 11.0 us)
Async XLA Ops:
  7.2 80.1 %copy-start = (bf16[512,2048]{1,0:T(8,128)(2,1)S(1)}, bf16[512,2048]{1,0:T(8,128)(2,1)}, u32[]{:S(2)}) copy-start(bf16[512,2048]{1,0:T(8,128)(2,1)} %param.24) | copy-start | bytes 6291460
  7.2 7.8 %copy-start.5 = (bf16[128,2304]{1,0:T(8,128)(2,1)S(1)}, bf16[128,2304]{1,0:T(8,128)(2,1)}, u32[]{:S(2)}) copy-start(bf16[128,2304]{1,0:T(8,128)(2,1)} %param.16) | copy-start | bytes 1769476
  7.2 49.4 %all-gather.10.cloned.1.call-start = ((), (), s32[]{:S(2)}) async-start(), calls=%async_computation.8 | async-start | bytes 3981312 | tf_op jit(solution)/shard_map/all_gather | solution.py:69
  12.2 83.3 %reduce-scatter.4.cloned.1.call-start = ((), (), s32[]{:S(2)}) async-start(), calls=%async_computation.3 | async-start | bytes 786432 | tf_op jit(solution)/shard_map/reduce_scatter | solution.py:119
  80.8 1.5 copy-start.3
  87.2 1.6 copy-start.8
  87.2 8.3 %copy-start.7 = (bf16[128,2048]{1,0:T(8,128)(2,1)S(1)}, bf16[128,2048]{1,0:T(8,128)(2,1)}, u32[]{:S(2)}) copy-start(bf16[128,2048]{1,0:T(8,128)(2,1)} %param.15) | copy-start | bytes 1572868
  88.5 40.7 %all-gather.6.cloned.1.call-start = ((), (), s32[]{:S(2)}) async-start(), calls=%async_computation.4 | async-start | bytes 1310720 | tf_op jit(solution)/shard_map/all_gather | solution.py:131
  96.6 37.5 %copy-start.4 = (bf16[128,1024]{1,0:T(8,128)(2,1)}, bf16[128,1024]{1,0:T(8,128)(2,1)S(1)}, u32[]{:S(2)}) copy-start(bf16[128,1024]{1,0:T(8,128)(2,1)S(1)} %get-tuple-element.3) | copy-start | bytes 786436
  100.0 40.8 %all-gather.8.cloned.1.call-start = ((), (), s32[]{:S(2)}) async-start(), calls=%async_computation.5 | async-start | bytes 3145728 | tf_op jit(solution)/shard_map/all_gather | solution.py:132
  129.2 76.1 %reduce-scatter.6.cloned.1.call-start = ((), (), s32[]{:S(2)}) async-start(), calls=%async_computation.6 | async-start | bytes 3145728 | tf_op jit(solution)/shard_map/reduce_scatter | solution.py:172
  134.1 6.7 %copy-start.6 = (bf16[2048,32]{0,1:T(8,128)(2,1)S(1)}, bf16[2048,32]{0,1:T(8,128)(2,1)}, u32[]{:S(2)}) copy-start(bf16[2048,32]{0,1:T(8,128)(2,1)} %param.26) | copy-start | bytes 393220
  148.9 2.0 copy-start.2
  190.6 45.8 %copy-start.1 = (bf16[512,2048]{1,0:T(8,128)(2,1)S(1)}, bf16[512,2048]{1,0:T(8,128)(2,1)}, u32[]{:S(2)}) copy-start(bf16[512,2048]{1,0:T(8,128)(2,1)} %param.24) | copy-start | bytes 6291460
  194.4 42.0 %reduce-scatter.8.cloned.1.call-start = ((), (), s32[]{:S(2)}) async-start(), calls=%async_computation.7 | async-start | bytes 1310720 | tf_op jit(solution)/shard_map/reduce_scatter | solution.py:173
Sparse Core Ops, SparseCore 0:
  12.3 44.2 all-gather.9
  88.7 6.7 reduce-scatter.3
  100.1 29.0 all-gather.5
  130.7 10.0 all-gather.7
  194.5 10.7 reduce-scatter.5
  208.1 28.3 reduce-scatter.7
where the time goes:
time: 244 us; the launch traced here: 243 us
  waiting for transfers between devices  114 us (47%)
  matrix products  54.4 us (22%)
  local copies, waits for them, and re-layouts  35.3 us (14%)
  other arithmetic  21.8 us (9%)
  between operations  14.5 us (6%)
  blocking collectives  2.47 us (1%)
    all_gather x1, waiting for transfers between devices, local(): gathered = lax.all_gather(share, ('exp', 'ffn'), axis=0, tiled=False)  35.9 us
    reduce_scatter x1, waiting for transfers between devices, local(): moe_out = lax.psum_scatter(moe_cols, 'exp', scatter_dimension=0, tiled=True)  31.1 us
    all_gather x1, waiting for transfers between devices, local(): normed_half = lax.all_gather(normed_cols, 'exp', axis=0, tiled=True)  29.2 us
    dot_general x1, matrix products, local(): jnp.einsum('jmf,jfd->jmd', active, down_weight, preferred_element_type=jn...  23.6 us
    dot_general x1, matrix products, local(): jnp.einsum('jmd,jdf->jmf', grouped, gate_weight, preferred_element_type=j...  12.3 us
    reduce_scatter x1, waiting for transfers between devices, local(): moe_cols = lax.psum_scatter(mixture, 'ffn', scatter_dimension=1, tiled=True)  10.9 us
    gather x2, local copies, waits for them, and re-layouts, local(): jnp.take(flat_pages, key_rows, axis=0).reshape(CMAX + fresh_len, QKD)  10.1 us
    unnamed x22, local copies, waits for them, and re-layouts  9.92 us
  transfers between devices with their start and end apart: 6, of which 6 were waited for; matrix products, arithmetic and copies ran while one was open for 8% of the time, Pallas kernels for 0%

commit v1 on v0

--- a/solution.py
+++ b/solution.py
@@ -128,7 +128,31 @@
     normed_cols = (
         hidden_wide * lax.rsqrt(mean_square + EPSILON) * gain_cols.astype(jnp.float32)
     ).astype(jnp.bfloat16)
-    normed_half = lax.all_gather(normed_cols, "exp", axis=0, tiled=True)
+    block_next = lax.axis_size("exp")
+    heard = lax.axis_index("exp")
+    kept_arr, carry, response = (block_next, heard, normed_cols.shape[0])
+    all_rows = jnp.zeros(
+        [pp * kept_arr if src_i == 0 else pp for src_i, pp in enumerate(normed_cols.shape)],
+        normed_cols.dtype,
+    )
+    normed_half = lax.dynamic_update_slice_in_dim(all_rows, normed_cols, carry * response, axis=0)
+    val = placed = normed_cols
+    ii = 1
+    while ii < kept_arr // 2 + 1:
+        val = lax.ppermute(
+            val, "exp", [(src_i, (src_i + 1) % kept_arr) for src_i in range(kept_arr)]
+        )
+        normed_half = lax.dynamic_update_slice_in_dim(
+            normed_half, val, (carry - ii) % kept_arr * response, axis=0
+        )
+        if 2 * ii < kept_arr:
+            placed = lax.ppermute(
+                placed, "exp", [(src_i, (src_i - 1) % kept_arr) for src_i in range(kept_arr)]
+            )
+            normed_half = lax.dynamic_update_slice_in_dim(
+                normed_half, placed, (carry + ii) % kept_arr * response, axis=0
+            )
+        ii += 1
     normed_all = lax.all_gather(normed_half, "ffn", axis=1, tiled=True)
     expert_ids = lax.broadcasted_iota(jnp.int32, (1, 1, EXPERTS), 2)
     route_hot = routes_all[:, :, None] == expert_ids

time: 244 us -> 235 us (0.963)
  waiting for transfers between devices: 114 us -> 101 us
  starting transfers between devices: 0.42 us -> 4.26 us
    all_gather x1 -> x0, waiting for transfers between devices: 29.2 us -> none  [local(): normed_half = lax.all_gather(normed_cols, 'exp', axis=0, tiled=True)]
    ppermute x0 -> x3, waiting for transfers between devices: none -> 17.8 us  [the longest x2 13 us: local(): lax.ppermute(val, 'exp', [(src_i, (src_i + 1) % kept_arr) for src_i in ra...]
    ppermute x0 -> x3, starting transfers between devices: none -> 3.88 us  [the longest x1 2.1 us: local(): lax.ppermute(placed, 'exp', [(src_i, (src_i - 1) % kept_arr) for src_i in...]
    unnamed x22 -> x24, local copies, waits for them, and re-layouts: 9.92 us -> 10.9 us
  transfers between devices with their start and end apart: 6 -> 8, of which waited for: 6 -> 7; matrix products, arithmetic and copies ran while one was open for 8% -> 8% of each run, Pallas kernels for 0% -> 0%
where the time goes in v1:
time: 235 us; the launch traced here: 234 us
  waiting for transfers between devices  101 us (43%)
  matrix products  54.4 us (23%)
  local copies, waits for them, and re-layouts  36.5 us (16%)
  other arithmetic  21.1 us (9%)
  between operations  14.2 us (6%)
  starting transfers between devices  4.26 us (2%)
  blocking collectives  2.47 us (1%)
    all_gather x1, waiting for transfers between devices, local(): gathered = lax.all_gather(share, ('exp', 'ffn'), axis=0, tiled=False)  35.9 us
    reduce_scatter x1, waiting for transfers between devices, local(): moe_out = lax.psum_scatter(moe_cols, 'exp', scatter_dimension=0, tiled=True)  31 us
    dot_general x1, matrix products, local(): jnp.einsum('jmf,jfd->jmd', active, down_weight, preferred_element_type=jn...  23.6 us
    ppermute x2, waiting for transfers between devices, local(): lax.ppermute(val, 'exp', [(src_i, (src_i + 1) % kept_arr) for src_i in ra...  13 us
    dot_general x1, matrix products, local(): jnp.einsum('jmd,jdf->jmf', grouped, gate_weight, preferred_element_type=j...  12.3 us
    unnamed x24, local copies, waits for them, and re-layouts  10.9 us
    gather x2, local copies, waits for them, and re-layouts, local(): jnp.take(flat_pages, key_rows, axis=0).reshape(CMAX + fresh_len, QKD)  10.1 us
    reduce_scatter x1, waiting for transfers between devices, local(): moe_cols = lax.psum_scatter(mixture, 'ffn', scatter_dimension=1, tiled=True)  9.91 us
  transfers between devices with their start and end apart: 8, of which 7 were waited for; matrix products, arithmetic and copies ran while one was open for 8% of the time, Pallas kernels for 0%

profile of v1, /device:TPU:0, one launch (start us, length us, event | category | flops | bytes accessed | tf_op | source)
XLA Modules:
  0.0 234.3 jit_solution(8121245977852328619)
XLA Ops:
  9.8 2.3 fusion.36
  16.3 1.3 copy.55
  18.3 1.3 iota_compare_fusion.6
  20.7 35.9 %all-gather.7.cloned.1.call-done = bf16[8,21,9216]{2,1,0:T(8,128)(2,1)} async-done(((bf16[1,21,9216]{2,1,0:T(8,128)(2,1)}), bf16[8,21,9216]{2,1,0:T(8,128)(2,1)}) %all-gather.7.cloned.1.call-update) | async-done | bytes 3096592 | tf_op jit(solution)/shard_map/all_gather | solution.py:69
  56.6 4.8 %reshape.369 = bf16[168,9216]{1,0:T(8,128)(2,1)} reshape(bf16[8,21,9216]{2,1,0:T(8,128)(2,1)} %all-gather.7.cloned.1.call-done) | data formatting | bytes 6193152
  61.4 6.3 %gather_fusion = bf16[80,9216]{1,0:T(8,128)(2,1)} fusion(bf16[168,9216]{1,0:T(8,128)(2,1)} %reshape.369, s32[1024]{0:T(1024)S(1)} %pad_clamp_fusion), kind=kCustom, calls=%fused_computation | custom fusion | bytes 2949440 | tf_op jit(solution)/shard_map/jit(_take)/gather | solution.py:92
  67.7 2.7 %broadcast_select_fusion = bf16[80,9216]{1,0:T(8,128)(2,1)} fusion(bf16[80,9216]{1,0:T(8,128)(2,1)} %gather_fusion, pred[80]{0:T(512)(128)(4,1)S(1)} %compare_and_fusion), kind=kLoop, calls=%fused_computation.21 | loop fusion | flops 737280 | bytes 2949200 | tf_op jit(solution)/shard_map/jit(_take)/select_n | solution.py:92
  70.3 3.9 %gather.7 = bf16[1280,576]{1,0:T(8,128)(2,1)} reshape(bf16[80,9216]{1,0:T(8,128)(2,1)} %gather_fusion) | data formatting | bytes 2949120 | tf_op jit(solution)/shard_map/jit(_take)/gather | solution.py:92
  74.2 3.9 %select_n.143 = bf16[1280,576]{1,0:T(8,128)(2,1)} reshape(bf16[80,9216]{1,0:T(8,128)(2,1)} %broadcast_select_fusion) | data formatting | bytes 2949120 | tf_op jit(solution)/shard_map/jit(_take)/select_n | solution.py:92
  78.1 2.6 %fusion.6 = f32[128,4,1280]{0,2,1:T(8,128)S(1)} fusion(bf16[128,4,576]{0,2,1:T(8,128)(2,1)S(1)} %bitcast.75, bf16[1280,576]{1,0:T(8,128)(2,1)} %select_n.143, pred[128,1280]{0,1:T(8,128)(4,1)S(1)} %and_or_fusion), kind=kOutput, calls=%fused_computation.13 | convolution fusion | flops 756285440 | bytes 4849664 | tf_op jit(solution)/shard_map/thd,kd->thk/dot_general | solution.py:97
  80.8 1.5 copy-done.4
  82.9 4.4 %fusion.23 = bf16[4,128,128]{1,2,0:T(8,128)(2,1)S(1)} fusion(bf16[512,4,128]{0,2,1:T(8,128)(2,1)S(1)} %bitcast.76, bf16[1280,576]{1,0:T(8,128)(2,1)} %gather.7, pred[1280]{0:T(1024)(128)(4,1)S(1)} %broadcast_in_dim.84, f32[128,4]{0,1:T(4,128)S(1)} %fusion.50, f32[128,4,1280]{0,2,1:T(8,128)} %copy-done.4), kind=kOutput, calls=%fused_computation.32 | convolution fusion | flops 741148416 | bytes 7212288 | tf_op jit(solution)/shard_map/thl,lhd->thd/dot_general | solution.py:113
  88.8 6.7 %reduce-scatter.4.cloned.1.call-done = bf16[128,1024]{1,0:T(8,128)(2,1)} async-done(((bf16[128,2048]{1,0:T(8,128)(2,1)}), bf16[128,1024]{1,0:T(8,128)(2,1)}) %reduce-scatter.4.cloned.1.call-update) | async-done | bytes 262160 | tf_op jit(solution)/shard_map/reduce_scatter | solution.py:119
  96.6 2.5 %psum.7 = f32[128,1]{0,1:T(1,128)S(1)} all-reduce(f32[128,1]{0,1:T(1,128)S(1)} %bitcast.79), channel_id=1, replica_groups=mesh['req'=4,'exp'=4,'ffn'=2] {'ffn'}, use_global_device_ids=true, to_apply=%region_7.8 | all-reduce | flops 128 | bytes 1024 | tf_op jit(solution)/shard_map/psum | solution.py:125
  99.4 1.8 collective-permute-start
  101.1 2.1 collective-permute-start.1
  103.2 7.1 %collective-permute-done = bf16[128,1024]{1,0:T(8,128)(2,1)S(1)} collective-permute-done((bf16[128,1024]{1,0:T(8,128)(2,1)S(1)}, bf16[128,1024]{1,0:T(8,128)(2,1)S(1)}, u32[]{:S(2)}, u32[]{:S(2)}) %collective-permute-start) | collective-permute-done | bytes 262176 | tf_op jit(solution)/shard_map/ppermute | solution.py:142
  110.4 4.8 %collective-permute-done.1 = bf16[128,1024]{1,0:T(8,128)(2,1)S(1)} collective-permute-done((bf16[128,1024]{1,0:T(8,128)(2,1)S(1)}, bf16[128,1024]{1,0:T(8,128)(2,1)S(1)}, u32[]{:S(2)}, u32[]{:S(2)}) %collective-permute-start.1) | collective-permute-done | bytes 262176 | tf_op jit(solution)/shard_map/ppermute | solution.py:149
  115.2 5.9 %collective-permute-done.2 = bf16[128,1024]{1,0:T(8,128)(2,1)S(1)} collective-permute-done((bf16[128,1024]{1,0:T(8,128)(2,1)S(1)}, bf16[128,1024]{1,0:T(8,128)(2,1)S(1)}, u32[]{:S(2)}, u32[]{:S(2)}) %collective-permute-start.2) | collective-permute-done | bytes 262176 | tf_op jit(solution)/shard_map/ppermute | solution.py:142
  122.3 4.7 %reshape.351 = bf16[4,42,9216]{2,1,0:T(8,128)(2,1)} reshape(bf16[8,21,9216]{2,1,0:T(8,128)(2,1)} %all-gather.7.cloned.1.call-done) | data formatting | bytes 6193152 | tf_op jit(solution)/shard_map/reshape | solution.py:70
  129.4 2.3 fusion.2
  131.7 1.4 fusion.1
  133.1 2.3 fusion.52
  135.6 1.7 select_reduce_fusion
  137.3 3.9 %convolution_convert_fusion = bf16[1024,2048]{1,0:T(8,128)(2,1)S(1)} fusion(pred[1024,512]{1,0:T(8,128)(4,1)S(1)} %fusion.2, bf16[512,2048]{1,0:T(8,128)(2,1)} %all-gather.5.cloned.1.call-done), kind=kOutput, calls=%fused_computation.9 | convolution fusion | flops 2149580800 | bytes 6815744 | tf_op jit(solution)/shard_map/dot_general | solution.py:186
  141.2 2.0 copy-done.2
  143.2 12.3 %fusion.51 = f32[8,128,704]{1,2,0:T(8,128)} fusion(bf16[8,128,2048]{2,1,0:T(8,128)(2,1)S(1)} %bitcast.73, bf16[8,2048,704]{1,2,0:T(8,128)(2,1)} %param.27), kind=kOutput, calls=%fused_computation.93 | convolution fusion | flops 2952790016 | bytes 30146560 | tf_op jit(solution)/shard_map/jmd,jdf->jmf/dot_general | solution.py:188
  155.5 23.6 %fusion.8 = f32[8,128,2048]{2,1,0:T(8,128)} fusion(bf16[8,704,2048]{2,1,0:T(8,128)(2,1)} %param.29, f32[8,128,704]{1,2,0:T(8,128)} %fusion.51, bf16[8,128,2048]{2,1,0:T(8,128)(2,1)} %bitcast.74, bf16[8,2048,704]{1,2,0:T(8,128)(2,1)} %param.28), kind=kOutput, calls=%fused_computation.19 | convolution fusion | flops 5909905408 | bytes 61603840 | tf_op jit(solution)/shard_map/jmf,jfd->jmd/dot_general | solution.py:191
  179.1 3.9 %fusion.3 = bf16[1024,2048]{1,0:T(8,128)(2,1)S(1)} fusion(f32[8,128,2048]{2,1,0:T(8,128)} %fusion.8, f32[1024]{0:T(1024)S(1)} %select_reduce_fusion), kind=kLoop, calls=%fused_computation.8 | loop fusion | flops 4194304 | bytes 12587008 | tf_op jit(solution)/shard_map/convert_element_type | solution.py:192
  183.0 3.8 %convolution_convert_fusion.1 = bf16[512,2048]{1,0:T(8,128)(2,1)} fusion(pred[512,1024]{1,0:T(8,128)(4,1)S(1)} %fusion.1, bf16[1024,2048]{1,0:T(8,128)(2,1)S(1)} %fusion.3), kind=kOutput, calls=%fused_computation.15 | convolution fusion | flops 2148532224 | bytes 6815744 | tf_op jit(solution)/shard_map/dot_general | solution.py:195
  186.8 9.9 %reduce-scatter.6.cloned.1.call-done = bf16[512,1024]{1,0:T(8,128)(2,1)} async-done(((bf16[512,2048]{1,0:T(8,128)(2,1)}), bf16[512,1024]{1,0:T(8,128)(2,1)}) %reduce-scatter.6.cloned.1.call-update) | async-done | bytes 1048592 | tf_op jit(solution)/shard_map/reduce_scatter | solution.py:196
  196.7 31.0 %reduce-scatter.8.cloned.1.call-done = bf16[128,1024]{1,0:T(8,128)(2,1)} async-done(((bf16[512,1024]{1,0:T(8,128)(2,1)}), bf16[128,1024]{1,0:T(8,128)(2,1)}) %reduce-scatter.8.cloned.1.call-update) | async-done | bytes 262160 | tf_op jit(solution)/shard_map/reduce_scatter | solution.py:197
  (83 shorter events, 15.8 us)
Async XLA Ops:
  7.2 80.1 %copy-start = (bf16[512,2048]{1,0:T(8,128)(2,1)S(1)}, bf16[512,2048]{1,0:T(8,128)(2,1)}, u32[]{:S(2)}) copy-start(bf16[512,2048]{1,0:T(8,128)(2,1)} %param.24) | copy-start | bytes 6291460
  7.2 7.8 %copy-start.6 = (bf16[128,2304]{1,0:T(8,128)(2,1)S(1)}, bf16[128,2304]{1,0:T(8,128)(2,1)}, u32[]{:S(2)}) copy-start(bf16[128,2304]{1,0:T(8,128)(2,1)} %param.16) | copy-start | bytes 1769476
  7.2 49.4 %all-gather.7.cloned.1.call-start = ((), (), s32[]{:S(2)}) async-start(), calls=%async_computation.7 | async-start | bytes 3981312 | tf_op jit(solution)/shard_map/all_gather | solution.py:69
  12.2 83.3 %reduce-scatter.4.cloned.1.call-start = ((), (), s32[]{:S(2)}) async-start(), calls=%async_computation.3 | async-start | bytes 786432 | tf_op jit(solution)/shard_map/reduce_scatter | solution.py:119
  80.8 1.5 copy-start.4
  87.2 1.6 copy-start.9
  87.2 8.3 %copy-start.8 = (bf16[128,2048]{1,0:T(8,128)(2,1)S(1)}, bf16[128,2048]{1,0:T(8,128)(2,1)}, u32[]{:S(2)}) copy-start(bf16[128,2048]{1,0:T(8,128)(2,1)} %param.15) | copy-start | bytes 1572868
  88.5 44.6 %all-gather.5.cloned.1.call-start = ((), (), s32[]{:S(2)}) async-start(), calls=%async_computation.4 | async-start | bytes 3145728 | tf_op jit(solution)/shard_map/all_gather | solution.py:156
  96.6 30.3 %copy-start.5 = (bf16[128,1024]{1,0:T(8,128)(2,1)}, bf16[128,1024]{1,0:T(8,128)(2,1)S(1)}, u32[]{:S(2)}) copy-start(bf16[128,1024]{1,0:T(8,128)(2,1)S(1)} %get-tuple-element.5) | copy-start | bytes 786436
  99.4 11.0 %collective-permute-start = (bf16[128,1024]{1,0:T(8,128)(2,1)S(1)}, bf16[128,1024]{1,0:T(8,128)(2,1)S(1)}, u32[]{:S(2)}, u32[]{:S(2)}) collective-permute-start(bf16[128,1024]{1,0:T(8,128)(2,1)S(1)} %get-tuple-element.3), channel_id=1, source_target_pairs={{0,2},{2,4},{4,6},{6,0},{1,3},{3,5},{5,7},{7,1},{8,10},{10,12},{12... | collective-permute-start | bytes 786440 | tf_op jit(solution)/shard_map/ppermute | solution.py:142
  101.1 14.0 %collective-permute-start.1 = (bf16[128,1024]{1,0:T(8,128)(2,1)S(1)}, bf16[128,1024]{1,0:T(8,128)(2,1)S(1)}, u32[]{:S(2)}, u32[]{:S(2)}) collective-permute-start(bf16[128,1024]{1,0:T(8,128)(2,1)S(1)} %get-tuple-element.3), channel_id=1, source_target_pairs={{0,6},{2,0},{4,2},{6,4},{1,7},{3,1},{5,3},{7,5},{8,14},{10,8},{12,... | collective-permute-start | bytes 786440 | tf_op jit(solution)/shard_map/ppermute | solution.py:149
  110.4 10.7 %collective-permute-start.2 = (bf16[128,1024]{1,0:T(8,128)(2,1)S(1)}, bf16[128,1024]{1,0:T(8,128)(2,1)S(1)}, u32[]{:S(2)}, u32[]{:S(2)}) collective-permute-start(bf16[128,1024]{1,0:T(8,128)(2,1)S(1)} %collective-permute-done), channel_id=1, source_target_pairs={{0,2},{2,4},{4,6},{6,0},{1,3},{3,5},{5,7},{7,1},{8,10},{10,12},{12... | collective-permute-start | bytes 786440 | tf_op jit(solution)/shard_map/ppermute | solution.py:142
  121.1 1.0 copy-start.3
  122.1 74.6 %reduce-scatter.6.cloned.1.call-start = ((), (), s32[]{:S(2)}) async-start(), calls=%async_computation.5 | async-start | bytes 3145728 | tf_op jit(solution)/shard_map/reduce_scatter | solution.py:196
  127.0 6.1 %copy-start.7 = (bf16[2048,32]{0,1:T(8,128)(2,1)S(1)}, bf16[2048,32]{0,1:T(8,128)(2,1)}, u32[]{:S(2)}) copy-start(bf16[2048,32]{0,1:T(8,128)(2,1)} %param.26) | copy-start | bytes 393220
  141.2 2.0 copy-start.2
  183.0 44.8 %copy-start.1 = (bf16[512,2048]{1,0:T(8,128)(2,1)S(1)}, bf16[512,2048]{1,0:T(8,128)(2,1)}, u32[]{:S(2)}) copy-start(bf16[512,2048]{1,0:T(8,128)(2,1)} %param.24) | copy-start | bytes 6291460
  186.7 41.0 %reduce-scatter.8.cloned.1.call-start = ((), (), s32[]{:S(2)}) async-start(), calls=%async_computation.6 | async-start | bytes 1310720 | tf_op jit(solution)/shard_map/reduce_scatter | solution.py:197
Sparse Core Ops, SparseCore 0:
  12.3 44.2 all-gather.6
  88.7 6.7 reduce-scatter.3
  122.2 9.8 all-gather.4
  186.9 9.7 reduce-scatter.5
  199.4 28.3 reduce-scatter.7
